TPU v7x, 32 devices: a whole 2x2x4 slice. The times are simulated.
32 devices in a mesh: ctx: 16 (over z, y, x), tp: 2 (over core).
Axes of the slice: x: 2, y: 2, z: 4, core: 2. Of those that a mesh axis runs over, the one named last changes fastest.
Arguments:
- x_act: bfloat16 [4096, 8192], P('ctx', 'tp'), may hold values from -0.119628906 to 0.119628906
- b_proj: bfloat16 [4096, 128], P('ctx'), may hold values from -0.5 to 0.5
- c_proj: bfloat16 [4096, 128], P('ctx'), may hold values from -0.5 to 0.5
- dt_raw: bfloat16 [4096, 128], P('ctx', 'tp'), may hold values from -3 to 3
- a_log: float32 [128], P('tp'), may hold values from -12 to -2
- d_skip: float32 [128], P('tp'), may hold values from 0.5 to 2
- grad_out: bfloat16 [4096, 8192], P('ctx', 'tp'), may hold values from -6 to 6
Outputs:
- grad_x: bfloat16 [4096, 8192], P('ctx', 'tp')
- grad_b: float32 [4096, 128], P('ctx')
- grad_c: float32 [4096, 128], P('ctx')
- grad_dt: bfloat16 [4096, 128], P('ctx', 'tp')
All inputs are finite; a program needn't handle non-finite values.
Results may differ from a plain program's by a relative error of at most 0.001.
Values may be sent and summed in bfloat16 or wider, within the bound.
No kernel may reach another device: no remote copies, remote signals or barrier semaphores. Data moves between devices by JAX's collectives and lax.ppermute only.
A program may use at most 192 MiB of HBM per device.

v0:
```python
from functools import partial
import jax
import jax.numpy as jnp
from jax import lax
from jax.sharding import PartitionSpec as P

BLOCK = 256
precise = lax.Precision.HIGH


def head_forward(x_head, b_rows, c_rows, raw_step, log_rate, skip_gain, start_state, block_len):
    length, head_width = x_head.shape
    blocks = length // block_len
    step_size = jax.nn.softplus(raw_step)
    decay_rates = -jnp.exp(log_rate) * step_size
    row_index = lax.broadcasted_iota(jnp.int32, (block_len, block_len), 0)
    col_index = lax.broadcasted_iota(jnp.int32, (block_len, block_len), 1)
    lower_mask = row_index >= col_index
    running = jnp.dot(
        decay_rates.reshape(blocks, block_len), lower_mask.astype(jnp.float32).T, precision=precise
    )
    between = jnp.where(lower_mask[None], running[:, :, None] - running[:, None, :], -1e30)
    x_blocks = x_head.reshape(blocks, block_len, head_width)
    b_blocks = b_rows.reshape(blocks, block_len, -1)
    c_blocks = c_rows.reshape(blocks, block_len, -1)
    s_blocks = step_size.reshape(blocks, block_len)
    scores = (
        jnp.einsum("kin,kjn->kij", c_blocks, b_blocks, precision=precise)
        * jnp.exp(between)
        * s_blocks[:, None, :]
    )
    output = jnp.einsum("kij,kjp->kip", scores, x_blocks, precision=precise)
    closing = running[:, -1]
    weighted = (jnp.exp(closing[:, None] - running) * s_blocks)[:, :, None] * x_blocks
    states = jnp.einsum("kjp,kjn->kpn", weighted, b_blocks, precision=precise)
    block_rows = lax.broadcasted_iota(jnp.int32, (blocks, blocks), 0)
    block_cols = lax.broadcasted_iota(jnp.int32, (blocks, blocks), 1)
    through = jnp.dot((block_rows >= block_cols).astype(jnp.float32), closing, precision=precise)
    before = through - closing
    carry_weight = jnp.exp(
        jnp.where(block_rows > block_cols, before[:, None] - through[None, :], -1e30)
    )
    entering = (
        jnp.einsum("kj,jpn->kpn", carry_weight, states, precision=precise)
        + jnp.exp(before)[:, None, None] * start_state[None]
    )
    reading = jnp.exp(running)[:, :, None] * c_blocks
    output = output + jnp.einsum("kin,kpn->kip", reading, entering, precision=precise)
    output = output.reshape(length, head_width) + skip_gain * x_head
    final_state = (
        jnp.einsum("j,jpn->pn", jnp.exp(through[-1] - through), states, precision=precise)
        + jnp.exp(through[-1]) * start_state
    )
    return (output, final_state)


N_CHUNKS = 1


def chunk_backward(x_seq, g_seq, raw_seq, b_rows, c_rows, rate, gain):
    length = x_seq.shape[0]
    heads = raw_seq.shape[1]
    head_width = x_seq.shape[1] // heads
    runner = partial(head_forward, block_len=BLOCK)
    mapped = jax.vmap(runner, in_axes=(0, None, None, 0, 0, 0, 0))
    x_heads = x_seq.astype(jnp.float32).reshape(length, heads, head_width).transpose(1, 0, 2)
    g_heads = g_seq.astype(jnp.float32).reshape(length, heads, head_width).transpose(1, 0, 2)
    raw_heads = raw_seq.astype(jnp.float32).T
    anchor = jnp.zeros((heads, head_width, b_rows.shape[1]), jnp.float32)

    def forward(x_val, b_val, c_val, raw_val):
        return mapped(x_val, b_val, c_val, raw_val, rate, gain, anchor)[0]

    _, pullback = jax.vjp(forward, x_heads, b_rows, c_rows, raw_heads)
    grad_xh, grad_b_all, grad_c_all, grad_raw = pullback(g_heads)
    x_back = grad_xh.transpose(1, 0, 2).reshape(length, heads * head_width).astype(jnp.bfloat16)
    raw_back = grad_raw.T
    return (x_back, raw_back, grad_b_all, grad_c_all)


def gather_ctx(block, owners, me):
    if owners & owners - 1:
        return lax.all_gather(block, "ctx", axis=0, tiled=True)
    have = block
    step = 1
    while step < owners:
        theirs = lax.ppermute(have, "ctx", [(k, k ^ step) for k in range(owners)])
        upper = me // step % 2 == 1
        have = jnp.where(upper, jnp.concatenate([theirs, have]), jnp.concatenate([have, theirs]))
        step *= 2
    return have


def local(x_act, b_proj, c_proj, dt_raw, a_log, d_skip, grad_out):
    rows = x_act.shape[0]
    heads_here = dt_raw.shape[1]
    head_width = x_act.shape[1] // heads_here
    state = b_proj.shape[1]
    owners = lax.axis_size("ctx")
    per_owner = heads_here // owners
    chunks = N_CHUNKS if per_owner % N_CHUNKS == 0 else 1
    per_chunk = per_owner // chunks
    me = lax.axis_index("ctx")
    half = lax.axis_index("tp")
    own_seq = gather_ctx(jnp.where(half == 0, b_proj, c_proj), owners, me)
    other_seq = lax.ppermute(own_seq, "tp", [(0, 1), (1, 0)])
    b_rows = jnp.where(half == 0, own_seq, other_seq).astype(jnp.float32)
    c_rows = jnp.where(half == 0, other_seq, own_seq).astype(jnp.float32)
    first_head = me * per_owner
    rate_own = lax.dynamic_slice_in_dim(a_log, first_head, per_owner)
    gain_own = lax.dynamic_slice_in_dim(d_skip, first_head, per_owner)
    x4 = x_act.reshape(rows, owners, per_owner, head_width)
    g4 = grad_out.reshape(rows, owners, per_owner, head_width)
    r3 = dt_raw.reshape(rows, owners, per_owner)
    x_parts, raw_parts = ([], [])
    grad_b_all = None
    grad_c_all = None
    for c in range(chunks):
        sl = slice(c * per_chunk, (c + 1) * per_chunk)
        width = per_chunk * head_width
        x_in = x4[:, :, sl, :].reshape(rows, owners, width)
        g_in = g4[:, :, sl, :].reshape(rows, owners, width)
        if c == 0:
            g_in, _ = lax.optimization_barrier((g_in, own_seq))
        x_seq = lax.all_to_all(x_in, "ctx", split_axis=1, concat_axis=0, tiled=True).reshape(
            rows * owners, width
        )
        g_seq = lax.all_to_all(g_in, "ctx", split_axis=1, concat_axis=0, tiled=True).reshape(
            rows * owners, width
        )
        raw_seq = lax.all_to_all(
            r3[:, :, sl], "ctx", split_axis=1, concat_axis=0, tiled=True
        ).reshape(rows * owners, per_chunk)
        x_back, raw_back, gb, gc = chunk_backward(
            x_seq, g_seq, raw_seq, b_rows, c_rows, rate_own[sl], gain_own[sl]
        )
        x_parts.append(
            lax.all_to_all(x_back, "ctx", split_axis=0, concat_axis=1, tiled=True).reshape(
                rows, owners, 1, width
            )
        )
        raw_parts.append(raw_back)
        grad_b_all = gb if grad_b_all is None else grad_b_all + gb
        grad_c_all = gc if grad_c_all is None else grad_c_all + gc
    grad_x = jnp.concatenate(x_parts, axis=2).reshape(rows, owners * per_owner * head_width)
    raw_all = jnp.concatenate(raw_parts, axis=1)
    is_first = half == 0
    send = jnp.where(is_first, grad_c_all, grad_b_all)
    keep = jnp.where(is_first, grad_b_all, grad_c_all)
    mine = keep + lax.ppermute(send, "tp", [(0, 1), (1, 0)])
    steps_back = raw_all.reshape(owners, rows, per_owner).transpose(0, 2, 1)
    extra = per_owner * rows // state
    if extra * state == per_owner * rows:
        packed = jnp.concatenate(
            [mine.reshape(owners, rows, state), steps_back.reshape(owners, extra, state)], axis=1
        )
        parts = lax.all_to_all(packed, "ctx", split_axis=0, concat_axis=0, tiled=True)
        mine = parts[:, :rows, :].sum(axis=0)
        got_dt = parts[:, rows:, :].reshape(owners, per_owner, rows)
    else:
        parts = lax.all_to_all(
            mine.reshape(owners, rows, state), "ctx", split_axis=0, concat_axis=0, tiled=True
        )
        mine = parts.sum(axis=0)
        got_dt = lax.all_to_all(steps_back, "ctx", split_axis=0, concat_axis=0, tiled=True)
    grad_dt = got_dt.transpose(2, 0, 1).reshape(rows, heads_here).astype(jnp.bfloat16)
    other = lax.ppermute(mine, "tp", [(0, 1), (1, 0)])
    grad_b = jnp.where(is_first, mine, other)
    grad_c = jnp.where(is_first, other, mine)
    return (grad_x, grad_b, grad_c, grad_dt)


def solution(mesh):
    in_specs = (
        P("ctx", "tp"),
        P("ctx", None),
        P("ctx", None),
        P("ctx", "tp"),
        P("tp"),
        P("tp"),
        P("ctx", "tp"),
    )
    out_specs = (P("ctx", "tp"), P("ctx", None), P("ctx", None), P("ctx", "tp"))
    return jax.shard_map(local, mesh=mesh, in_specs=in_specs, out_specs=out_specs, check_vma=False)
```

profile of v0, /device:TPU:12, one launch (start us, length us, event | category | flops | bytes accessed | tf_op | source)
XLA Modules:
  0.0 329.9 jit_solution(7301412444082762005)
XLA Ops:
  2.0 7.2 %all-to-all-start.1 = ((bf16[256,16,4]{0,2,1:T(4,128)(2,1)}), bf16[256,16,4]{0,2,1:T(4,128)(2,1)S(1)}, u32[]{:S(2)}, u32[]{:S(2)}) async-start(bf16[256,16,4]{0,2,1:T(4,128)(2,1)} %reshape.136), calls=%async_computation.1 | async-start | bytes 65536 | tf_op jit(solution)/shard_map/all_to_all | solution.py:131
  9.2 4.1 %copy.83 = bf16[256,4096]{0,1:T(8,128)(2,1)} copy(bf16[256,4096]{1,0:T(8,128)(2,1)} %param.7) | data formatting | bytes 4194304 | tf_op args[0]
  14.4 5.9 %all-to-all-start.3 = ((bf16[256,16,256]{0,2,1:T(8,128)(2,1)}), bf16[256,16,256]{0,2,1:T(8,128)(2,1)S(1)}, u32[]{:S(2)}, u32[]{:S(2)}) async-start(bf16[256,16,256]{0,2,1:T(8,128)(2,1)} %bitcast.189), calls=%async_computation.3 | async-start | bytes 4194304 | tf_op jit(solution)/shard_map/all_to_all | solution.py:125
  21.9 6.7 %collective-permute-done = bf16[256,128]{1,0:T(8,128)(2,1)S(1)} collective-permute-done((bf16[256,128]{1,0:T(8,128)(2,1)S(1)}, bf16[256,128]{1,0:T(8,128)(2,1)S(1)}, u32[]{:S(2)}, u32[]{:S(2)}) %collective-permute-start) | collective-permute-done | bytes 65568 | tf_op jit(solution)/shard_map/ppermute | solution.py:87
  29.5 4.9 %collective-permute-done.1 = bf16[512,128]{1,0:T(8,128)(2,1)S(1)} collective-permute-done((bf16[512,128]{1,0:T(8,128)(2,1)S(1)}, bf16[512,128]{1,0:T(8,128)(2,1)S(1)}, u32[]{:S(2)}, u32[]{:S(2)}) %collective-permute-start.1) | collective-permute-done | bytes 131104 | tf_op jit(solution)/shard_map/ppermute | solution.py:87
  34.5 2.6 collective-permute-start.2
  37.2 22.8 %collective-permute-done.2 = bf16[1024,128]{1,0:T(8,128)(2,1)S(1)} collective-permute-done((bf16[1024,128]{1,0:T(8,128)(2,1)S(1)}, bf16[1024,128]{1,0:T(8,128)(2,1)S(1)}, u32[]{:S(2)}, u32[]{:S(2)}) %collective-permute-start.2) | collective-permute-done | bytes 262176 | tf_op jit(solution)/shard_map/ppermute | solution.py:87
  60.2 3.5 %collective-permute-start.3 = (bf16[2048,128]{1,0:T(8,128)(2,1)S(1)}, bf16[2048,128]{1,0:T(8,128)(2,1)}, u32[]{:S(2)}, u32[]{:S(2)}) collective-permute-start(bf16[2048,128]{1,0:T(8,128)(2,1)S(1)} %maximum_select_fusion.1), channel_id=1, source_target_pairs={{0,16},{2,18},{4,20},{6,22},{8,24},{10,26},{12,28},{14,30},{16,0},... | collective-permute-start | bytes 1572872 | tf_op jit(solution)/shard_map/ppermute | solution.py:87
  63.7 4.1 %copy.70 = bf16[256,4096]{0,1:T(8,128)(2,1)} copy(bf16[256,4096]{1,0:T(8,128)(2,1)} %param.13) | data formatting | bytes 4194304 | tf_op args[6]
  67.8 20.4 %collective-permute-done.3 = bf16[2048,128]{1,0:T(8,128)(2,1)} collective-permute-done((bf16[2048,128]{1,0:T(8,128)(2,1)S(1)}, bf16[2048,128]{1,0:T(8,128)(2,1)}, u32[]{:S(2)}, u32[]{:S(2)}) %collective-permute-start.3) | collective-permute-done | bytes 524320 | tf_op jit(solution)/shard_map/ppermute | solution.py:87
  90.1 8.1 %all-to-all-start = ((bf16[256,16,256]{0,2,1:T(8,128)(2,1)}), bf16[256,16,256]{0,2,1:T(8,128)(2,1)}, u32[]{:S(2)}, u32[]{:S(2)}) async-start(bf16[256,16,256]{0,2,1:T(8,128)(2,1)} %bitcast.190), calls=%async_computation | async-start | bytes 4194304 | tf_op jit(solution)/shard_map/all_to_all | solution.py:128
  102.9 2.8 fusion.112
  105.7 2.5 copy.84
  108.2 2.9 reshape.142
  111.1 33.6 %all-to-all-done = bf16[256,16,256]{0,2,1:T(8,128)(2,1)} async-done(((bf16[256,16,256]{0,2,1:T(8,128)(2,1)}), bf16[256,16,256]{0,2,1:T(8,128)(2,1)}, u32[]{:S(2)}, u32[]{:S(2)}) %all-to-all-start) | async-done | bytes 2097184 | tf_op jit(solution)/shard_map/all_to_all | solution.py:128
  144.7 4.1 %copy.71 = bf16[16,256,1,256]{1,0,3,2:T(8,128)(2,1)} copy(bf16[16,256,1,256]{1,3,0,2:T(8,128)(2,1)} %bitcast.2) | data formatting | bytes 4194304 | tf_op jit(solution)/shard_map/all_to_all | solution.py:128
  148.8 4.2 %reshape.135 = bf16[4096,4,64]{0,2,1:T(8,128)(2,1)} reshape(bf16[16,256,1,256]{1,0,3,2:T(8,128)(2,1)} %copy.71) | data formatting | bytes 4194304 | tf_op jit(solution)/shard_map/reshape | solution.py:128
  153.0 5.9 %multiply_reduce_fusion.4 = (f32[4,16]{1,0:T(4,128)}, f32[4,16,64,128]{3,2,1,0:T(8,128)S(1)}) fusion(f32[16,256,128]{1,2,0:T(8,128)} %copy.73, f32[4,16,256]{2,1,0:T(8,128)S(1)} %get-tuple-element.36, bf16[4,8,16,8,256]{4,3,2,1,0:T(8,128)(2,1)} %bitcast.179), kind=kOutput, calls=%fused_computation.42 | convolution fusion | flops 808452032 | bytes 6357248 | tf_op jit(solution)/shard_map/transpose(jvp(vmap(kin,kpn->kip)))/dot_general | solution.py:48
  160.9 4.0 %fusion.10 = (f32[4,16,256]{2,0,1:T(4,128)S(1)}, f32[16,4,64,256]{3,2,1,0:T(8,128)}) fusion(bf16[4,8,16,8,256]{4,3,2,1,0:T(8,128)(2,1)S(1)} %bitcast.171, bf16[16,256,128,1]{2,1,3,0:T(8,128)(2,1)S(1)} %bitcast.176, f32[16,4,64,128]{3,0,2,1:T(8,128)S(1)} %fusion.44), kind=kOutput, calls=%fused_computation.18 | convolution fusion | flops 808435712 | bytes 9502720 | tf_op jit(solution)/shard_map/transpose(jvp(vmap(kjp,kjn->kpn)))/dot_general | solution.py:35
  164.9 16.5 %fusion.5 = (f32[4,16,256]{2,1,0:T(8,128)}, f32[4,16,256]{2,1,0:T(8,128)}, f32[4,16,256]{2,1,0:T(8,128)S(1)}, f32[16,256,256]{2,1,0:T(8,128)}, f32[4,16,256,256]{3,2,1,0:T(8,128)}) fusion(f32[4,16,256]{2,1,0:T(8,128)S(1)} %bitcast.204, f32[4,16,256]{2,1,0:T(8,128)S(1)} %get-tuple-element.37, f32[16,256,256]{2,1,0:T(8,128)S(1)} %copy-done.12, ...), kind=kOutput, calls=%fused_computation.9 | convolution fusion | flops 594493440 | bytes 29753344 | tf_op jit(solution)/shard_map/transpose(jvp(vmap(kij,kjp->kip)))/dot_general | solution.py:32
  182.3 5.2 %fusion.9 = f32[16,256,128,1]{2,1,3,0:T(8,128)} fusion(f32[4,16,256]{2,0,1:T(4,128)S(1)} %copy.72, f32[16,4,64,128]{3,0,2,1:T(8,128)S(1)} %fusion.44, bf16[4,8,16,8,256]{4,3,2,1,0:T(8,128)(2,1)S(1)} %bitcast.173), kind=kOutput, calls=%fused_computation.17 | convolution fusion | flops 807403520 | bytes 6356992 | tf_op jit(solution)/shard_map/transpose(jvp(vmap(kjp,kjn->kpn)))/dot_general | solution.py:35
  192.2 5.1 %multiply_reduce_fusion.3 = (f32[16,256,128]{1,2,0:T(8,128)}, f32[4,16,256]{2,1,0:T(8,128)}) fusion(f32[4,16,256]{2,1,0:T(8,128)S(1)} %copy-done.18, f32[16,256,128]{1,2,0:T(8,128)S(1)} %copy-done.13, f32[4,16,64,128]{3,1,2,0:T(8,128)S(1)} %fusion.47, bf16[4,8,16,8,256]{4,3,2,1,0:T(8,128)(2,1)S(1)} %bitcast.181), kind=kOutput, calls=%fused_computation.11 | convolution fusion | flops 813154304 | bytes 8519680 | tf_op jit(solution)/shard_map/transpose(jvp(vmap(kin,kpn->kip)))/dot_general | solution.py:48
  197.3 2.1 copy.93
  199.4 3.7 %convolution_add_fusion = f32[16,256,128]{2,1,0:T(8,128)S(1)} fusion(f32[16,256,128]{2,1,0:T(8,128)S(1)} %copy.93, f32[16,256,256]{2,1,0:T(8,128)} %get-tuple-element.17, bf16[16,256,128]{2,1,0:T(8,128)(2,1)S(1)} %bitcast.178), kind=kOutput, calls=%fused_computation.57 | convolution fusion | flops 805830656 | bytes 9437184 | tf_op jit(solution)/shard_map/transpose(jvp(vmap(kin,kjn->kij)))/dot_general | solution.py:28
  203.8 3.8 %broadcast_select_fusion.1 = (f32[16,256,128]{2,1,0:T(8,128)S(1)}, f32[16,256,128]{2,1,0:T(8,128)}) fusion(f32[16,256,128]{2,1,0:T(8,128)S(1)} %convolution_add_fusion, pred[]{:T(512)S(6)} %eq.35, f32[16,256,256]{2,1,0:T(8,128)S(1)} %copy-done.4, bf16[16,256,128]{2,1,0:T(8,128)(2,1)S(1)} %bitcast.186, f32[16,256,128,1]{2,1,3,0:T(8,128)S(1)} %copy-done.11), kind=kOutput, calls=%fused_computation.72 | convolution fusion | flops 806879232 | bytes 13631489 | tf_op jit(solution)/shard_map/transpose(jvp(vmap(kin,kjn->kij)))/dot_general | solution.py:28
  207.7 3.7 %fusion.110 = (f32[4,16]{1,0:T(4,128)S(1)}, f32[4,16]{1,0:T(4,128)S(1)}) fusion(f32[4,16]{1,0:T(4,128)S(1)} %get-tuple-element.38, f32[4,16]{1,0:T(4,128)S(1)} %get-tuple-element.23, f32[16,4,64,128]{3,2,1,0:T(8,128)S(1)} %copy-done.1, f32[4,16,64,128]{3,2,1,0:T(8,128)S(1)} %copy-done.10, pred[16,16]{1,0:T(8,128)(4,1)S(1)} %iota_compare_fusion.6), kind=kOutput, calls=%fused_computation.136 | convolution fusion | flops 50337664 | bytes 4195584 | tf_op jit(solution)/shard_map/transpose(jvp(vmap(kj,jpn->kpn)))/dot_general | solution.py:44
  215.6 5.7 %all-to-all-start.4 = ((f32[16,264,128]{2,1,0:T(8,128)}), f32[16,264,128]{2,1,0:T(8,128)}, u32[]{:S(2)}, u32[]{:S(2)}) async-start(f32[16,264,128]{2,1,0:T(8,128)} %pad_maximum_fusion), calls=%async_computation.4 | async-start | bytes 4325376 | tf_op jit(solution)/shard_map/all_to_all | solution.py:157
  221.3 9.0 %fusion.12 = f32[16,4,8,8,256]{4,3,2,1,0:T(8,128)S(1)} fusion(f32[16,4,64,256]{3,2,1,0:T(8,128)} %get-tuple-element.40, f32[4,16,256]{2,0,1:T(4,128)S(1)} %copy.72, bf16[4,8,16,8,256]{4,3,2,1,0:T(8,128)(2,1)S(1)} %bitcast.182, f32[4,16,256,256]{3,2,1,0:T(8,128)} %get-tuple-element.24), kind=kOutput, calls=%fused_computation.21 | convolution fusion | flops 1612709888 | bytes 27328512 | tf_op jit(solution)/shard_map/transpose(jvp(vmap(kij,kjp->kip)))/dot_general | solution.py:32
  234.3 36.7 %all-to-all-done.4 = f32[16,264,128]{2,1,0:T(8,128)} async-done(((f32[16,264,128]{2,1,0:T(8,128)}), f32[16,264,128]{2,1,0:T(8,128)}, u32[]{:S(2)}, u32[]{:S(2)}) %all-to-all-start.4) | async-done | bytes 2162720 | tf_op jit(solution)/shard_map/all_to_all | solution.py:157
  271.0 5.7 %all-to-all-start.2 = ((bf16[16,256,256]{1,2,0:T(8,128)(2,1)}), bf16[16,256,256]{1,2,0:T(8,128)(2,1)S(1)}, u32[]{:S(2)}, u32[]{:S(2)}) async-start(bf16[16,256,256]{1,2,0:T(8,128)(2,1)} %copy.82), calls=%async_computation.2 | async-start | bytes 4194304 | tf_op jit(solution)/shard_map/all_to_all | solution.py:138
  278.5 46.1 %all-to-all-done.2 = bf16[16,256,256]{1,2,0:T(8,128)(2,1)S(1)} async-done(((bf16[16,256,256]{1,2,0:T(8,128)(2,1)}), bf16[16,256,256]{1,2,0:T(8,128)(2,1)S(1)}, u32[]{:S(2)}, u32[]{:S(2)}) %all-to-all-start.2) | async-done | bytes 2097184 | tf_op jit(solution)/shard_map/all_to_all | solution.py:138
  324.6 2.8 copy.99
  (111 shorter events, 32.1 us)
Async XLA Ops:
  2.0 12.4 %all-to-all-start.1 = ((bf16[256,16,4]{0,2,1:T(4,128)(2,1)}), bf16[256,16,4]{0,2,1:T(4,128)(2,1)S(1)}, u32[]{:S(2)}, u32[]{:S(2)}) async-start(bf16[256,16,4]{0,2,1:T(4,128)(2,1)} %reshape.136), calls=%async_computation.1 | async-start | bytes 65536 | tf_op jit(solution)/shard_map/all_to_all | solution.py:131
  14.4 6.0 %copy-start.15 = (bf16[256,128]{1,0:T(8,128)(2,1)S(1)}, bf16[256,128]{1,0:T(8,128)(2,1)}, u32[]{:S(2)}) copy-start(bf16[256,128]{1,0:T(8,128)(2,1)} %param.8) | copy-start | bytes 196612
  14.4 6.0 %copy-start.16 = (bf16[256,128]{1,0:T(8,128)(2,1)S(1)}, bf16[256,128]{1,0:T(8,128)(2,1)}, u32[]{:S(2)}) copy-start(bf16[256,128]{1,0:T(8,128)(2,1)} %param.9) | copy-start | bytes 196612
  14.4 75.7 %all-to-all-start.3 = ((bf16[256,16,256]{0,2,1:T(8,128)(2,1)}), bf16[256,16,256]{0,2,1:T(8,128)(2,1)S(1)}, u32[]{:S(2)}, u32[]{:S(2)}) async-start(bf16[256,16,256]{0,2,1:T(8,128)(2,1)} %bitcast.189), calls=%async_computation.3 | async-start | bytes 4194304 | tf_op jit(solution)/shard_map/all_to_all | solution.py:125
  20.4 8.2 %collective-permute-start = (bf16[256,128]{1,0:T(8,128)(2,1)S(1)}, bf16[256,128]{1,0:T(8,128)(2,1)S(1)}, u32[]{:S(2)}, u32[]{:S(2)}) collective-permute-start(bf16[256,128]{1,0:T(8,128)(2,1)S(1)} %broadcast_select_fusion.6), channel_id=1, source_target_pairs={{0,2},{2,0},{4,6},{6,4},{8,10},{10,8},{12,14},{14,12},{16,18},{18,... | collective-permute-start | bytes 196616 | tf_op jit(solution)/shard_map/ppermute | solution.py:87
  28.7 5.8 %collective-permute-start.1 = (bf16[512,128]{1,0:T(8,128)(2,1)S(1)}, bf16[512,128]{1,0:T(8,128)(2,1)S(1)}, u32[]{:S(2)}, u32[]{:S(2)}) collective-permute-start(bf16[512,128]{1,0:T(8,128)(2,1)S(1)} %maximum_select_fusion.3), channel_id=1, source_target_pairs={{0,4},{2,6},{4,0},{6,2},{8,12},{10,14},{12,8},{14,10},{16,20},{18,... | collective-permute-start | bytes 393224 | tf_op jit(solution)/shard_map/ppermute | solution.py:87
  34.5 25.5 %collective-permute-start.2 = (bf16[1024,128]{1,0:T(8,128)(2,1)S(1)}, bf16[1024,128]{1,0:T(8,128)(2,1)S(1)}, u32[]{:S(2)}, u32[]{:S(2)}) collective-permute-start(bf16[1024,128]{1,0:T(8,128)(2,1)S(1)} %maximum_select_fusion.2), channel_id=1, source_target_pairs={{0,8},{2,10},{4,12},{6,14},{8,0},{10,2},{12,4},{14,6},{16,24},{18,... | collective-permute-start | bytes 786440 | tf_op jit(solution)/shard_map/ppermute | solution.py:87
  60.2 7.7 %copy-start.14 = (bf16[2048,128]{1,0:T(8,128)(2,1)}, bf16[2048,128]{1,0:T(8,128)(2,1)S(1)}, u32[]{:S(2)}) copy-start(bf16[2048,128]{1,0:T(8,128)(2,1)S(1)} %maximum_select_fusion.1) | copy-start | bytes 1572868
  60.2 28.0 %collective-permute-start.3 = (bf16[2048,128]{1,0:T(8,128)(2,1)S(1)}, bf16[2048,128]{1,0:T(8,128)(2,1)}, u32[]{:S(2)}, u32[]{:S(2)}) collective-permute-start(bf16[2048,128]{1,0:T(8,128)(2,1)S(1)} %maximum_select_fusion.1), channel_id=1, source_target_pairs={{0,16},{2,18},{4,20},{6,22},{8,24},{10,26},{12,28},{14,30},{16,0},... | collective-permute-start | bytes 1572872 | tf_op jit(solution)/shard_map/ppermute | solution.py:87
  90.1 8.2 %copy-start.27 = (f32[64]{0:T(128)S(1)}, f32[64]{0:T(128)}, u32[]{:S(2)}) copy-start(f32[64]{0:T(128)} %param.11) | copy-start | bytes 772
  90.1 8.1 %copy-start.7 = (bf16[256,16,256]{0,2,1:T(8,128)(2,1)}, bf16[256,16,256]{0,2,1:T(8,128)(2,1)S(1)}, u32[]{:S(2)}) copy-start(bf16[256,16,256]{0,2,1:T(8,128)(2,1)S(1)} %all-to-all-done.3) | copy-start | bytes 6291460
  90.1 54.6 %all-to-all-start = ((bf16[256,16,256]{0,2,1:T(8,128)(2,1)}), bf16[256,16,256]{0,2,1:T(8,128)(2,1)}, u32[]{:S(2)}, u32[]{:S(2)}) async-start(bf16[256,16,256]{0,2,1:T(8,128)(2,1)} %bitcast.190), calls=%async_computation | async-start | bytes 4194304 | tf_op jit(solution)/shard_map/all_to_all | solution.py:128
  98.4 2.7 collective-permute-start.4
  99.4 53.6 %copy-start.17 = (f32[4,16,256]{2,1,0:T(8,128)}, f32[4,16,256]{2,1,0:T(8,128)S(1)}, u32[]{:S(2)}) copy-start(f32[4,16,256]{2,1,0:T(8,128)S(1)} %get-tuple-element.36) | copy-start | bytes 196612
  101.2 4.5 %copy-start.5 = (bf16[4096,128]{1,0:T(8,128)(2,1)}, bf16[4096,128]{1,0:T(8,128)(2,1)S(1)}, u32[]{:S(2)}) copy-start(bf16[4096,128]{1,0:T(8,128)(2,1)S(1)} %get-tuple-element.27) | copy-start | bytes 3145732
  160.9 4.0 %copy-start.2 = (bf16[4096,4,64]{0,2,1:T(8,128)(2,1)S(1)}, bf16[4096,4,64]{0,2,1:T(8,128)(2,1)}, u32[]{:S(2)}) copy-start(bf16[4096,4,64]{0,2,1:T(8,128)(2,1)} %reshape.135) | copy-start | bytes 6291460
  160.9 4.0 %copy-start.12 = (f32[16,256,256]{2,1,0:T(8,128)S(1)}, f32[16,256,256]{2,1,0:T(8,128)}, u32[]{:S(2)}) copy-start(f32[16,256,256]{2,1,0:T(8,128)} %fusion.112) | copy-start | bytes 12582916
  160.9 4.0 %copy-start.22 = (f32[1,4,16,256]{3,2,1,0:T(8,128)S(1)}, f32[1,4,16,256]{3,2,1,0:T(8,128)}, u32[]{:S(2)}) copy-start(f32[1,4,16,256]{3,2,1,0:T(8,128)} %copy.227) | copy-start | bytes 196612
  199.4 4.4 %copy-start.11 = (f32[16,256,128,1]{2,1,3,0:T(8,128)S(1)}, f32[16,256,128,1]{2,1,3,0:T(8,128)}, u32[]{:S(2)}) copy-start(f32[16,256,128,1]{2,1,3,0:T(8,128)} %fusion.9) | copy-start | bytes 6291460
  203.8 3.9 %copy-start.1 = (f32[16,4,64,128]{3,2,1,0:T(8,128)S(1)}, f32[16,4,64,128]{3,2,1,0:T(8,128)}, u32[]{:S(2)}) copy-start(f32[16,4,64,128]{3,2,1,0:T(8,128)} %copy-done) | copy-start | bytes 6291460
  203.8 3.9 %copy-start.10 = (f32[4,16,64,128]{3,2,1,0:T(8,128)S(1)}, f32[4,16,64,128]{3,2,1,0:T(8,128)}, u32[]{:S(2)}) copy-start(f32[4,16,64,128]{3,2,1,0:T(8,128)} %copy-done.9) | copy-start | bytes 6291460
  207.6 3.8 %copy-start.29 = (f32[4,16]{1,0:T(4,128)S(1)}, f32[4,16]{1,0:T(4,128)}, u32[]{:S(2)}) copy-start(f32[4,16]{1,0:T(4,128)} %get-tuple-element.41) | copy-start | bytes 772
  207.6 4.1 %copy-start.19 = (f32[4,16,256]{2,1,0:T(8,128)S(1)}, f32[4,16,256]{2,1,0:T(8,128)}, u32[]{:S(2)}) copy-start(f32[4,16,256]{2,1,0:T(8,128)} %get-tuple-element.14) | copy-start | bytes 196612
  207.6 4.1 %copy-start.20 = (f32[4,16,256]{2,1,0:T(8,128)S(1)}, f32[4,16,256]{2,1,0:T(8,128)}, u32[]{:S(2)}) copy-start(f32[4,16,256]{2,1,0:T(8,128)} %get-tuple-element.15) | copy-start | bytes 196612
  207.6 4.1 %copy-start.21 = (f32[4,16,256]{2,1,0:T(8,128)S(1)}, f32[4,16,256]{2,1,0:T(8,128)}, u32[]{:S(2)}) copy-start(f32[4,16,256]{2,1,0:T(8,128)} %get-tuple-element.19) | copy-start | bytes 196612
  207.6 4.4 %copy-start.26 = (f32[4]{0:T(128)S(1)}, f32[4]{0:T(128)}, u32[]{:S(2)}) copy-start(f32[4]{0:T(128)} %copy-done.25) | copy-start | bytes 52
  207.6 4.6 %collective-permute-start.5 = (f32[4096,128]{1,0:T(8,128)}, f32[4096,128]{1,0:T(8,128)}, u32[]{:S(2)}, u32[]{:S(2)}) collective-permute-start(f32[4096,128]{1,0:T(8,128)} %bitcast.34), channel_id=1, source_target_pairs={{0,1},{1,0},{2,3},{3,2},{4,5},{5,4},{6,7},{7,6},{8,9},{9,8},{10,11... | collective-permute-start | bytes 6291464 | tf_op jit(solution)/shard_map/ppermute | solution.py:150
  215.6 5.7 %copy-start.28 = (f32[64]{0:T(128)S(1)}, f32[64]{0:T(128)}, u32[]{:S(2)}) copy-start(f32[64]{0:T(128)} %param.12) | copy-start | bytes 772
  215.6 5.8 %copy-start.3 = (bf16[4096,4,64]{0,2,1:T(8,128)(2,1)S(1)}, bf16[4096,4,64]{0,2,1:T(8,128)(2,1)}, u32[]{:S(2)}) copy-start(bf16[4096,4,64]{0,2,1:T(8,128)(2,1)} %reshape.135) | copy-start | bytes 6291460
  215.6 55.4 %all-to-all-start.4 = ((f32[16,264,128]{2,1,0:T(8,128)}), f32[16,264,128]{2,1,0:T(8,128)}, u32[]{:S(2)}, u32[]{:S(2)}) async-start(f32[16,264,128]{2,1,0:T(8,128)} %pad_maximum_fusion), calls=%async_computation.4 | async-start | bytes 4325376 | tf_op jit(solution)/shard_map/all_to_all | solution.py:157
  271.0 53.6 %all-to-all-start.2 = ((bf16[16,256,256]{1,2,0:T(8,128)(2,1)}), bf16[16,256,256]{1,2,0:T(8,128)(2,1)S(1)}, u32[]{:S(2)}, u32[]{:S(2)}) async-start(bf16[16,256,256]{1,2,0:T(8,128)(2,1)} %copy.82), calls=%async_computation.2 | async-start | bytes 4194304 | tf_op jit(solution)/shard_map/all_to_all | solution.py:138
  278.4 50.5 %collective-permute-start.6 = (f32[256,128]{1,0:T(8,128)S(1)}, f32[256,128]{1,0:T(8,128)S(1)}, u32[]{:S(2)}, u32[]{:S(2)}) collective-permute-start(f32[256,128]{1,0:T(8,128)S(1)} %slice_reduce_fusion), channel_id=1, source_target_pairs={{0,1},{1,0},{2,3},{3,2},{4,5},{5,4},{6,7},{7,6},{8,9},{9,8},{10,11... | collective-permute-start | bytes 393224 | tf_op jit(solution)/shard_map/ppermute | solution.py:167
  (10 other events, 24.9 us)
where the time goes:
time: 333 us; the launch traced here: 330 us
  waiting for transfers between devices  173 us (52%)
  matrix products  66.2 us (20%)
  starting transfers between devices  41.4 us (12%)
  local copies, waits for them, and re-layouts  37.9 us (11%)
  other arithmetic  9.84 us (3%)
    ppermute x4, waiting for transfers between devices, gather_ctx(): theirs = lax.ppermute(have, 'ctx', [(k, k ^ step) for k in range(owners)])  54.9 us
    all_to_all x1, waiting for transfers between devices, local(): lax.all_to_all(x_back, 'ctx', split_axis=0, concat_axis=1, tiled=True)  46.1 us
    all_to_all x1, waiting for transfers between devices, local(): lax.all_to_all(packed, 'ctx', split_axis=0, concat_axis=0, tiled=True)  36.7 us
    all_to_all x1, waiting for transfers between devices, local(): lax.all_to_all(g_in, 'ctx', split_axis=1, concat_axis=0, tiled=True)  33.6 us
    dot_general x2, matrix products, head_forward(): output = jnp.einsum('kij,kjp->kip', scores, x_blocks, precision=precise)  25.5 us
    unnamed x67, local copies, waits for them, and re-layouts  14.5 us
    dot_general x2, matrix products, head_forward(): jnp.einsum('kin,kpn->kip', reading, entering, precision=precise)  11 us
    dot_general x3, matrix products, head_forward(): states = jnp.einsum('kjp,kjn->kpn', weighted, b_blocks, precision=precise)  10.5 us
  transfers between devices with their start and end apart: 12, of which 9 were waited for; matrix products, arithmetic and copies ran while one was open for 14% of the time, Pallas kernels for 0%

commit v1 on v0

--- a/solution.py
+++ b/solution.py
@@ -6,6 +6,29 @@
 
 BLOCK = 256
 precise = lax.Precision.HIGH
+
+
+def cut_along(shard, dim, count):
+    shape = shard.shape
+    pieces = shard.reshape(*shape[:dim], count, shape[dim] // count, *shape[dim + 1 :])
+    return jnp.moveaxis(pieces, dim, 0)
+
+
+def in_order(tiles, dim):
+    dims = list(tiles.shape[1:])
+    dims[dim] *= tiles.shape[0]
+    return jnp.moveaxis(tiles, 0, dim).reshape(dims)
+
+
+def swapped_with_each(x, axis, split_dim, concat_dim):
+    size, here = (lax.axis_size(axis), lax.axis_index(axis))
+    blocks = cut_along(x, split_dim, size)
+    gathered = [blocks[here]]
+    for step in range(1, size):
+        sent = blocks[here ^ step]
+        gathered.append(lax.ppermute(sent, axis, [(i, i ^ step) for i in range(size)]))
+    blocks = jnp.stack(gathered)[here ^ jnp.arange(size)]
+    return in_order(blocks, concat_dim)
 
 
 def head_forward(x_head, b_rows, c_rows, raw_step, log_rate, skip_gain, start_state, block_len):
@@ -134,11 +157,7 @@
         x_back, raw_back, gb, gc = chunk_backward(
             x_seq, g_seq, raw_seq, b_rows, c_rows, rate_own[sl], gain_own[sl]
         )
-        x_parts.append(
-            lax.all_to_all(x_back, "ctx", split_axis=0, concat_axis=1, tiled=True).reshape(
-                rows, owners, 1, width
-            )
-        )
+        x_parts.append(swapped_with_each(x_back, "ctx", 0, 1).reshape(rows, owners, 1, width))
         raw_parts.append(raw_back)
         grad_b_all = gb if grad_b_all is None else grad_b_all + gb
         grad_c_all = gc if grad_c_all is None else grad_c_all + gc

time: 333 us -> 348 us (1.045)
  the two profiles are of different devices: /device:TPU:12 before, /device:TPU:9 now
where the time goes in v1:
time: 348 us; the launch traced here: 345 us
  waiting for transfers between devices  131 us (38%)
  local copies, waits for them, and re-layouts  73.2 us (21%)
  matrix products  65.6 us (19%)
  starting transfers between devices  60.3 us (17%)
  other arithmetic  13.1 us (4%)
    ppermute x4, waiting for transfers between devices, gather_ctx(): theirs = lax.ppermute(have, 'ctx', [(k, k ^ step) for k in range(owners)])  57 us
    ppermute x15, waiting for transfers between devices, swapped_with_each(): lax.ppermute(sent, axis, [(i, i ^ step) for i in range(size)])  43 us
    unnamed x89, local copies, waits for them, and re-layouts  31 us
    all_to_all x1, waiting for transfers between devices, local(): lax.all_to_all(g_in, 'ctx', split_axis=1, concat_axis=0, tiled=True)  29.6 us
    dot_general x2, matrix products, head_forward(): output = jnp.einsum('kij,kjp->kip', scores, x_blocks, precision=precise)  24.1 us
    ppermute x15, starting transfers between devices, swapped_with_each(): lax.ppermute(sent, axis, [(i, i ^ step) for i in range(size)])  20.6 us
    dynamic_slice x16, local copies, waits for them, and re-layouts, swapped_with_each(): sent = blocks[here ^ step]  12.9 us
    dot_general x3, matrix products, head_forward(): jnp.einsum('kin,kjn->kij', c_blocks, b_blocks, precision=precise)  11 us
  transfers between devices with their start and end apart: 26, of which 17 were waited for; matrix products, arithmetic and copies ran while one was open for 24% of the time, Pallas kernels for 0%

profile of v1, /device:TPU:9, one launch (start us, length us, event | category | flops | bytes accessed | tf_op | source)
XLA Modules:
  0.0 344.8 jit_solution(3173415457969885157)
XLA Ops:
  2.0 6.7 %all-to-all-start.1 = ((bf16[256,16,4]{0,2,1:T(4,128)(2,1)}), bf16[256,16,4]{0,2,1:T(4,128)(2,1)S(1)}, u32[]{:S(2)}, u32[]{:S(2)}) async-start(bf16[256,16,4]{0,2,1:T(4,128)(2,1)} %reshape.150), calls=%async_computation.1 | async-start | bytes 65536 | tf_op jit(solution)/shard_map/all_to_all | solution.py:154
  8.7 4.1 %copy.131 = bf16[256,4096]{0,1:T(8,128)(2,1)} copy(bf16[256,4096]{1,0:T(8,128)(2,1)} %param.7) | data formatting | bytes 4194304 | tf_op args[0]
  13.9 5.4 %all-to-all-start.2 = ((bf16[256,16,256]{0,2,1:T(8,128)(2,1)}), bf16[256,16,256]{0,2,1:T(8,128)(2,1)S(1)}, u32[]{:S(2)}, u32[]{:S(2)}) async-start(bf16[256,16,256]{0,2,1:T(8,128)(2,1)} %bitcast.236), calls=%async_computation.2 | async-start | bytes 4194304 | tf_op jit(solution)/shard_map/all_to_all | solution.py:148
  20.5 6.9 %collective-permute-done = bf16[256,128]{1,0:T(8,128)(2,1)S(1)} collective-permute-done((bf16[256,128]{1,0:T(8,128)(2,1)S(1)}, bf16[256,128]{1,0:T(8,128)(2,1)S(1)}, u32[]{:S(2)}, u32[]{:S(2)}) %collective-permute-start) | collective-permute-done | bytes 65568 | tf_op jit(solution)/shard_map/ppermute | solution.py:110
  28.3 4.2 %collective-permute-done.1 = bf16[512,128]{1,0:T(8,128)(2,1)S(1)} collective-permute-done((bf16[512,128]{1,0:T(8,128)(2,1)S(1)}, bf16[512,128]{1,0:T(8,128)(2,1)S(1)}, u32[]{:S(2)}, u32[]{:S(2)}) %collective-permute-start.1) | collective-permute-done | bytes 131104 | tf_op jit(solution)/shard_map/ppermute | solution.py:110
  34.4 24.0 %collective-permute-done.2 = bf16[1024,128]{1,0:T(8,128)(2,1)S(1)} collective-permute-done((bf16[1024,128]{1,0:T(8,128)(2,1)S(1)}, bf16[1024,128]{1,0:T(8,128)(2,1)S(1)}, u32[]{:S(2)}, u32[]{:S(2)}) %collective-permute-start.2) | collective-permute-done | bytes 262176 | tf_op jit(solution)/shard_map/ppermute | solution.py:110
  59.8 4.1 %copy.102 = bf16[256,4096]{0,1:T(8,128)(2,1)} copy(bf16[256,4096]{1,0:T(8,128)(2,1)} %param.13) | data formatting | bytes 4194304 | tf_op args[6]
  63.9 21.8 %collective-permute-done.3 = bf16[2048,128]{1,0:T(8,128)(2,1)} collective-permute-done((bf16[2048,128]{1,0:T(8,128)(2,1)S(1)}, bf16[2048,128]{1,0:T(8,128)(2,1)}, u32[]{:S(2)}, u32[]{:S(2)}) %collective-permute-start.3) | collective-permute-done | bytes 524320 | tf_op jit(solution)/shard_map/ppermute | solution.py:110
  87.6 9.1 %all-to-all-start = ((bf16[256,16,256]{0,2,1:T(8,128)(2,1)}), bf16[256,16,256]{0,2,1:T(8,128)(2,1)}, u32[]{:S(2)}, u32[]{:S(2)}) async-start(bf16[256,16,256]{0,2,1:T(8,128)(2,1)} %bitcast.237), calls=%async_computation | async-start | bytes 4194304 | tf_op jit(solution)/shard_map/all_to_all | solution.py:151
  112.8 29.6 %all-to-all-done = bf16[256,16,256]{0,2,1:T(8,128)(2,1)} async-done(((bf16[256,16,256]{0,2,1:T(8,128)(2,1)}), bf16[256,16,256]{0,2,1:T(8,128)(2,1)}, u32[]{:S(2)}, u32[]{:S(2)}) %all-to-all-start) | async-done | bytes 2097184 | tf_op jit(solution)/shard_map/all_to_all | solution.py:151
  142.4 4.1 %copy.103 = bf16[16,256,1,256]{1,0,3,2:T(8,128)(2,1)} copy(bf16[16,256,1,256]{1,3,0,2:T(8,128)(2,1)} %bitcast.2) | data formatting | bytes 4194304 | tf_op jit(solution)/shard_map/all_to_all | solution.py:151
  146.4 4.2 %reshape.149 = bf16[4096,4,64]{0,2,1:T(8,128)(2,1)} reshape(bf16[16,256,1,256]{1,0,3,2:T(8,128)(2,1)} %copy.103) | data formatting | bytes 4194304 | tf_op jit(solution)/shard_map/reshape | solution.py:151
  150.7 5.9 %multiply_reduce_fusion.4 = (f32[4,16]{1,0:T(4,128)}, f32[4,16,64,128]{3,2,1,0:T(8,128)S(1)}) fusion(f32[16,256,128]{1,2,0:T(8,128)} %copy.105, f32[4,16,256]{2,1,0:T(8,128)S(1)} %get-tuple-element.52, bf16[4,8,16,8,256]{4,3,2,1,0:T(8,128)(2,1)} %bitcast.226), kind=kOutput, calls=%fused_computation.43 | convolution fusion | flops 808452032 | bytes 6357248 | tf_op jit(solution)/shard_map/transpose(jvp(vmap(kin,kpn->kip)))/dot_general | solution.py:71
  158.6 3.9 %fusion.10 = (f32[4,16,256]{2,0,1:T(4,128)S(1)}, f32[16,4,64,256]{3,2,1,0:T(8,128)}) fusion(bf16[4,8,16,8,256]{4,3,2,1,0:T(8,128)(2,1)S(1)} %bitcast.217, bf16[16,256,128,1]{2,1,3,0:T(8,128)(2,1)S(1)} %bitcast.222, f32[16,4,64,128]{3,0,2,1:T(8,128)S(1)} %fusion.44), kind=kOutput, calls=%fused_computation.19 | convolution fusion | flops 808435712 | bytes 9502720 | tf_op jit(solution)/shard_map/transpose(jvp(vmap(kjp,kjn->kpn)))/dot_general | solution.py:58
  162.5 16.3 %fusion.5 = (f32[4,16,256]{2,1,0:T(8,128)}, f32[4,16,256]{2,1,0:T(8,128)}, f32[4,16,256]{2,1,0:T(8,128)S(1)}, f32[16,256,256]{2,1,0:T(8,128)}, f32[4,16,256,256]{3,2,1,0:T(8,128)}) fusion(f32[4,16,256]{2,1,0:T(8,128)S(1)} %bitcast.264, f32[4,16,256]{2,1,0:T(8,128)S(1)} %get-tuple-element.53, f32[16,256,256]{2,1,0:T(8,128)S(1)} %copy-done.13, ...), kind=kOutput, calls=%fused_computation.10 | convolution fusion | flops 594493440 | bytes 29753344 | tf_op jit(solution)/shard_map/transpose(jvp(vmap(kij,kjp->kip)))/dot_general | solution.py:55
  181.0 5.2 %fusion.9 = f32[16,256,128,1]{2,1,3,0:T(8,128)} fusion(f32[4,16,256]{2,0,1:T(4,128)S(1)} %copy.104, f32[16,4,64,128]{3,0,2,1:T(8,128)S(1)} %fusion.44, bf16[4,8,16,8,256]{4,3,2,1,0:T(8,128)(2,1)S(1)} %bitcast.220), kind=kOutput, calls=%fused_computation.18 | convolution fusion | flops 807403520 | bytes 6356992 | tf_op jit(solution)/shard_map/transpose(jvp(vmap(kjp,kjn->kpn)))/dot_general | solution.py:58
  188.3 5.1 %multiply_reduce_fusion.3 = (f32[16,256,128]{1,2,0:T(8,128)}, f32[4,16,256]{2,1,0:T(8,128)}) fusion(f32[4,16,256]{2,1,0:T(8,128)S(1)} %copy-done.21, f32[16,256,128]{1,2,0:T(8,128)S(1)} %copy-done.14, f32[4,16,64,128]{3,1,2,0:T(8,128)S(1)} %fusion.47, bf16[4,8,16,8,256]{4,3,2,1,0:T(8,128)(2,1)S(1)} %bitcast.228), kind=kOutput, calls=%fused_computation.12 | convolution fusion | flops 813154304 | bytes 8519680 | tf_op jit(solution)/shard_map/transpose(jvp(vmap(kin,kpn->kip)))/dot_general | solution.py:71
  195.6 3.7 %convolution_add_fusion = f32[16,256,128]{2,1,0:T(8,128)S(1)} fusion(f32[16,256,128]{2,1,0:T(8,128)S(1)} %copy.141, f32[16,256,256]{2,1,0:T(8,128)} %get-tuple-element.17, bf16[16,256,128]{2,1,0:T(8,128)(2,1)S(1)} %bitcast.224), kind=kOutput, calls=%fused_computation.58 | convolution fusion | flops 805830656 | bytes 9437184 | tf_op jit(solution)/shard_map/transpose(jvp(vmap(kin,kjn->kij)))/dot_general | solution.py:51
  200.0 4.7 %broadcast_select_fusion.1 = (f32[16,256,128]{2,1,0:T(8,128)}, f32[16,256,128]{2,1,0:T(8,128)}) fusion(f32[16,256,128]{2,1,0:T(8,128)S(1)} %convolution_add_fusion, pred[]{:T(512)S(6)} %eq.35, f32[16,256,256]{2,1,0:T(8,128)S(1)} %copy-done.5, bf16[16,256,128]{2,1,0:T(8,128)(2,1)S(1)} %bitcast.233, f32[16,256,128,1]{2,1,3,0:T(8,128)S(1)} %copy-done.12), kind=kOutput, calls=%fused_computation.73 | convolution fusion | flops 806879232 | bytes 13631489 | tf_op jit(solution)/shard_map/transpose(jvp(vmap(kin,kjn->kij)))/dot_general | solution.py:51
  207.0 7.8 %fusion.12 = f32[16,4,8,8,256]{4,3,2,1,0:T(8,128)S(1)} fusion(f32[16,4,64,256]{3,2,1,0:T(8,128)S(1)} %copy-done.4, f32[4,16,256]{2,0,1:T(4,128)S(1)} %copy.104, bf16[4,8,16,8,256]{4,3,2,1,0:T(8,128)(2,1)S(1)} %bitcast.229, f32[4,16,256,256]{3,2,1,0:T(8,128)} %get-tuple-element.24), kind=kOutput, calls=%fused_computation.22 | convolution fusion | flops 1612709888 | bytes 27328512 | tf_op jit(solution)/shard_map/transpose(jvp(vmap(kij,kjp->kip)))/dot_general | solution.py:55
  218.6 3.7 %fusion.111 = (f32[4,16]{1,0:T(4,128)S(1)}, f32[4,16]{1,0:T(4,128)S(1)}) fusion(f32[4,16]{1,0:T(4,128)S(1)} %get-tuple-element.54, f32[4,16]{1,0:T(4,128)S(1)} %get-tuple-element.23, f32[16,4,64,128]{3,2,1,0:T(8,128)S(1)} %copy-done.1, f32[4,16,64,128]{3,2,1,0:T(8,128)S(1)} %copy-done.11, pred[16,16]{1,0:T(8,128)(4,1)S(1)} %iota_compare_fusion.6), kind=kOutput, calls=%fused_computation.172 | convolution fusion | flops 50337664 | bytes 4195584 | tf_op jit(solution)/shard_map/transpose(jvp(vmap(kj,jpn->kpn)))/dot_general | solution.py:67
  227.0 6.1 %all-to-all-start.3 = ((f32[16,264,128]{2,1,0:T(8,128)}), f32[16,264,128]{2,1,0:T(8,128)}, u32[]{:S(2)}, u32[]{:S(2)}) async-start(f32[16,264,128]{2,1,0:T(8,128)} %pad_maximum_fusion), calls=%async_computation.3 | async-start | bytes 4325376 | tf_op jit(solution)/shard_map/all_to_all | solution.py:176
  236.6 6.3 %constant_dynamic-slice_fusion = (bf16[1,256,256]{1,0,2:T(2,128)(2,1)S(1)}, bf16[1,256,256]{1,0,2:T(2,128)(2,1)S(1)}, bf16[1,256,256]{1,0,2:T(2,128)(2,1)S(1)}, ...) fusion(bf16[16,256,256]{1,0,2:T(8,128)(2,1)S(1)} %bitcast.225, ...), kind=kLoop, calls=%fused_computation.142 | loop fusion | bytes 4194368 | tf_op jit(solution)/shard_map/dynamic_slice | solution.py:28
  261.9 5.0 %collective-permute-done.7 = bf16[256,256]{1,0:T(8,128)(2,1)} collective-permute-done((bf16[256,256]{1,0:T(8,128)(2,1)}, bf16[256,256]{1,0:T(8,128)(2,1)}, u32[]{:S(2)}, u32[]{:S(2)}) %collective-permute-start.7) | collective-permute-done | bytes 131104 | tf_op jit(solution)/shard_map/ppermute | solution.py:29
  268.5 4.5 %collective-permute-done.8 = bf16[256,256]{1,0:T(8,128)(2,1)} collective-permute-done((bf16[256,256]{1,0:T(8,128)(2,1)}, bf16[256,256]{1,0:T(8,128)(2,1)}, u32[]{:S(2)}, u32[]{:S(2)}) %collective-permute-start.8) | collective-permute-done | bytes 131104 | tf_op jit(solution)/shard_map/ppermute | solution.py:29
  287.1 11.2 %collective-permute-done.12 = bf16[256,256]{1,0:T(8,128)(2,1)S(1)} collective-permute-done((bf16[256,256]{1,0:T(8,128)(2,1)S(1)}, bf16[256,256]{1,0:T(8,128)(2,1)S(1)}, u32[]{:S(2)}, u32[]{:S(2)}) %collective-permute-start.12) | collective-permute-done | bytes 131104 | tf_op jit(solution)/shard_map/ppermute | solution.py:29
  301.1 3.8 %collective-permute-start.18 = (bf16[256,256]{1,0:T(8,128)(2,1)S(1)}, bf16[256,256]{1,0:T(8,128)(2,1)S(1)}, u32[]{:S(2)}, u32[]{:S(2)}) collective-permute-start(bf16[256,256]{1,0:T(8,128)(2,1)S(1)} %bitcast.251), channel_id=1, source_target_pairs={{0,28},{2,30},{4,24},{6,26},{8,20},{10,22},{12,16},{14,18},{16,12}... | collective-permute-start | bytes 393224 | tf_op jit(solution)/shard_map/ppermute | solution.py:29
  307.9 3.2 collective-permute-done.15
  311.7 7.6 %collective-permute-done.16 = bf16[256,256]{1,0:T(8,128)(2,1)S(1)} collective-permute-done((bf16[256,256]{1,0:T(8,128)(2,1)S(1)}, bf16[256,256]{1,0:T(8,128)(2,1)S(1)}, u32[]{:S(2)}, u32[]{:S(2)}) %collective-permute-start.16) | collective-permute-done | bytes 131104 | tf_op jit(solution)/shard_map/ppermute | solution.py:29
  319.9 3.5 %collective-permute-done.17 = bf16[256,256]{1,0:T(8,128)(2,1)S(1)} collective-permute-done((bf16[256,256]{1,0:T(8,128)(2,1)S(1)}, bf16[256,256]{1,0:T(8,128)(2,1)S(1)}, u32[]{:S(2)}, u32[]{:S(2)}) %collective-permute-start.17) | collective-permute-done | bytes 131104 | tf_op jit(solution)/shard_map/ppermute | solution.py:29
  324.1 3.9 %collective-permute-done.18 = bf16[256,256]{1,0:T(8,128)(2,1)S(1)} collective-permute-done((bf16[256,256]{1,0:T(8,128)(2,1)S(1)}, bf16[256,256]{1,0:T(8,128)(2,1)S(1)}, u32[]{:S(2)}, u32[]{:S(2)}) %collective-permute-start.18) | collective-permute-done | bytes 131104 | tf_op jit(solution)/shard_map/ppermute | solution.py:29
  338.2 4.1 %copy.147 = bf16[256,4096]{1,0:T(8,128)(2,1)} copy(bf16[256,4096]{0,1:T(8,128)(2,1)} %bitcast.239) | data formatting | bytes 4194304
  (181 shorter events, 103.7 us)
Async XLA Ops:
  2.0 11.9 %all-to-all-start.1 = ((bf16[256,16,4]{0,2,1:T(4,128)(2,1)}), bf16[256,16,4]{0,2,1:T(4,128)(2,1)S(1)}, u32[]{:S(2)}, u32[]{:S(2)}) async-start(bf16[256,16,4]{0,2,1:T(4,128)(2,1)} %reshape.150), calls=%async_computation.1 | async-start | bytes 65536 | tf_op jit(solution)/shard_map/all_to_all | solution.py:154
  13.9 73.7 %all-to-all-start.2 = ((bf16[256,16,256]{0,2,1:T(8,128)(2,1)}), bf16[256,16,256]{0,2,1:T(8,128)(2,1)S(1)}, u32[]{:S(2)}, u32[]{:S(2)}) async-start(bf16[256,16,256]{0,2,1:T(8,128)(2,1)} %bitcast.236), calls=%async_computation.2 | async-start | bytes 4194304 | tf_op jit(solution)/shard_map/all_to_all | solution.py:148
  19.3 8.1 %collective-permute-start = (bf16[256,128]{1,0:T(8,128)(2,1)S(1)}, bf16[256,128]{1,0:T(8,128)(2,1)S(1)}, u32[]{:S(2)}, u32[]{:S(2)}) collective-permute-start(bf16[256,128]{1,0:T(8,128)(2,1)S(1)} %broadcast_select_fusion.6), channel_id=1, source_target_pairs={{0,2},{2,0},{4,6},{6,4},{8,10},{10,8},{12,14},{14,12},{16,18},{18,... | collective-permute-start | bytes 196616 | tf_op jit(solution)/shard_map/ppermute | solution.py:110
  27.5 5.0 %collective-permute-start.1 = (bf16[512,128]{1,0:T(8,128)(2,1)S(1)}, bf16[512,128]{1,0:T(8,128)(2,1)S(1)}, u32[]{:S(2)}, u32[]{:S(2)}) collective-permute-start(bf16[512,128]{1,0:T(8,128)(2,1)S(1)} %maximum_select_fusion.3), channel_id=1, source_target_pairs={{0,4},{2,6},{4,0},{6,2},{8,12},{10,14},{12,8},{14,10},{16,20},{18,... | collective-permute-start | bytes 393224 | tf_op jit(solution)/shard_map/ppermute | solution.py:110
  32.6 25.8 %collective-permute-start.2 = (bf16[1024,128]{1,0:T(8,128)(2,1)S(1)}, bf16[1024,128]{1,0:T(8,128)(2,1)S(1)}, u32[]{:S(2)}, u32[]{:S(2)}) collective-permute-start(bf16[1024,128]{1,0:T(8,128)(2,1)S(1)} %maximum_select_fusion.2), channel_id=1, source_target_pairs={{0,8},{2,10},{4,12},{6,14},{8,0},{10,2},{12,4},{14,6},{16,24},{18,... | collective-permute-start | bytes 786440 | tf_op jit(solution)/shard_map/ppermute | solution.py:110
  58.5 27.2 %collective-permute-start.3 = (bf16[2048,128]{1,0:T(8,128)(2,1)S(1)}, bf16[2048,128]{1,0:T(8,128)(2,1)}, u32[]{:S(2)}, u32[]{:S(2)}) collective-permute-start(bf16[2048,128]{1,0:T(8,128)(2,1)S(1)} %maximum_select_fusion.1), channel_id=1, source_target_pairs={{0,16},{2,18},{4,20},{6,22},{8,24},{10,26},{12,28},{14,30},{16,0},... | collective-permute-start | bytes 1572872 | tf_op jit(solution)/shard_map/ppermute | solution.py:110
  87.5 9.2 %copy-start.30 = (f32[64]{0:T(128)S(1)}, f32[64]{0:T(128)}, u32[]{:S(2)}) copy-start(f32[64]{0:T(128)} %param.12) | copy-start | bytes 772
  87.5 10.4 %copy-start.31 = (f32[64]{0:T(128)S(1)}, f32[64]{0:T(128)}, u32[]{:S(2)}) copy-start(f32[64]{0:T(128)} %param.11) | copy-start | bytes 772
  87.6 9.1 %copy-start.8 = (bf16[256,16,256]{0,2,1:T(8,128)(2,1)}, bf16[256,16,256]{0,2,1:T(8,128)(2,1)S(1)}, u32[]{:S(2)}) copy-start(bf16[256,16,256]{0,2,1:T(8,128)(2,1)S(1)} %all-to-all-done.2) | copy-start | bytes 6291460
  87.6 54.8 %all-to-all-start = ((bf16[256,16,256]{0,2,1:T(8,128)(2,1)}), bf16[256,16,256]{0,2,1:T(8,128)(2,1)}, u32[]{:S(2)}, u32[]{:S(2)}) async-start(bf16[256,16,256]{0,2,1:T(8,128)(2,1)} %bitcast.237), calls=%async_computation | async-start | bytes 4194304 | tf_op jit(solution)/shard_map/all_to_all | solution.py:151
  98.1 4.8 %collective-permute-start.4 = (bf16[4096,128]{1,0:T(8,128)(2,1)S(1)}, bf16[4096,128]{1,0:T(8,128)(2,1)S(1)}, u32[]{:S(2)}, u32[]{:S(2)}) collective-permute-start(bf16[4096,128]{1,0:T(8,128)(2,1)S(1)} %maximum_select_fusion), channel_id=1, source_target_pairs={{0,1},{1,0},{2,3},{3,2},{4,5},{5,4},{6,7},{7,6},{8,9},{9,8},{10,11... | collective-permute-start | bytes 3145736 | tf_op jit(solution)/shard_map/ppermute | solution.py:129
  101.5 49.1 %copy-start.20 = (f32[4,16,256]{2,1,0:T(8,128)}, f32[4,16,256]{2,1,0:T(8,128)S(1)}, u32[]{:S(2)}) copy-start(f32[4,16,256]{2,1,0:T(8,128)S(1)} %get-tuple-element.52) | copy-start | bytes 196612
  200.0 7.0 %copy-start.4 = (f32[16,4,64,256]{3,2,1,0:T(8,128)S(1)}, f32[16,4,64,256]{3,2,1,0:T(8,128)}, u32[]{:S(2)}) copy-start(f32[16,4,64,256]{3,2,1,0:T(8,128)} %get-tuple-element.56) | copy-start | bytes 12582916
  204.6 18.4 %collective-permute-start.20 = (f32[4096,128]{1,0:T(8,128)}, f32[4096,128]{1,0:T(8,128)}, u32[]{:S(2)}, u32[]{:S(2)}) collective-permute-start(f32[4096,128]{1,0:T(8,128)} %bitcast.65), channel_id=1, source_target_pairs={{0,1},{1,0},{2,3},{3,2},{4,5},{5,4},{6,7},{7,6},{8,9},{9,8},{10,11... | collective-permute-start | bytes 6291464 | tf_op jit(solution)/shard_map/ppermute | solution.py:169
  227.0 101.7 %all-to-all-start.3 = ((f32[16,264,128]{2,1,0:T(8,128)}), f32[16,264,128]{2,1,0:T(8,128)}, u32[]{:S(2)}, u32[]{:S(2)}) async-start(f32[16,264,128]{2,1,0:T(8,128)} %pad_maximum_fusion), calls=%async_computation.3 | async-start | bytes 4325376 | tf_op jit(solution)/shard_map/all_to_all | solution.py:176
  236.6 9.2 %copy-start.29 = (s32[16]{0:T(128)S(1)}, s32[16]{0:T(128)}, u32[]{:S(2)}) copy-start(s32[16]{0:T(128)} %fusion.105) | copy-start | bytes 196
  244.6 11.8 %collective-permute-start.5 = (bf16[256,256]{1,0:T(8,128)(2,1)}, bf16[256,256]{1,0:T(8,128)(2,1)}, u32[]{:S(2)}, u32[]{:S(2)}) collective-permute-start(bf16[256,256]{1,0:T(8,128)(2,1)} %bitcast.21), channel_id=1, source_target_pairs={{0,2},{2,0},{4,6},{6,4},{8,10},{10,8},{12,14},{14,12},{16,18},{18,... | collective-permute-start | bytes 393224 | tf_op jit(solution)/shard_map/ppermute | solution.py:29
  248.6 10.5 %collective-permute-start.6 = (bf16[256,256]{1,0:T(8,128)(2,1)}, bf16[256,256]{1,0:T(8,128)(2,1)}, u32[]{:S(2)}, u32[]{:S(2)}) collective-permute-start(bf16[256,256]{1,0:T(8,128)(2,1)} %bitcast.262), channel_id=1, source_target_pairs={{0,4},{2,6},{4,0},{6,2},{8,12},{10,14},{12,8},{14,10},{16,20},{18,... | collective-permute-start | bytes 393224 | tf_op jit(solution)/shard_map/ppermute | solution.py:29
  250.6 16.3 %collective-permute-start.7 = (bf16[256,256]{1,0:T(8,128)(2,1)}, bf16[256,256]{1,0:T(8,128)(2,1)}, u32[]{:S(2)}, u32[]{:S(2)}) collective-permute-start(bf16[256,256]{1,0:T(8,128)(2,1)} %bitcast.261), channel_id=1, source_target_pairs={{0,6},{2,4},{4,2},{6,0},{8,14},{10,12},{12,10},{14,8},{16,22},{18,... | collective-permute-start | bytes 393224 | tf_op jit(solution)/shard_map/ppermute | solution.py:29
  251.7 21.3 %collective-permute-start.8 = (bf16[256,256]{1,0:T(8,128)(2,1)}, bf16[256,256]{1,0:T(8,128)(2,1)}, u32[]{:S(2)}, u32[]{:S(2)}) collective-permute-start(bf16[256,256]{1,0:T(8,128)(2,1)} %bitcast.27), channel_id=1, source_target_pairs={{0,8},{2,10},{4,12},{6,14},{8,0},{10,2},{12,4},{14,6},{16,24},{18,... | collective-permute-start | bytes 393224 | tf_op jit(solution)/shard_map/ppermute | solution.py:29
  251.8 24.1 %collective-permute-start.9 = (bf16[256,256]{1,0:T(8,128)(2,1)S(1)}, bf16[256,256]{1,0:T(8,128)(2,1)}, u32[]{:S(2)}, u32[]{:S(2)}) collective-permute-start(bf16[256,256]{1,0:T(8,128)(2,1)S(1)} %bitcast.260), channel_id=1, source_target_pairs={{0,10},{2,8},{4,14},{6,12},{8,2},{10,0},{12,6},{14,4},{16,26},{18,... | collective-permute-start | bytes 393224 | tf_op jit(solution)/shard_map/ppermute | solution.py:29
  256.4 24.0 %collective-permute-start.10 = (bf16[256,256]{1,0:T(8,128)(2,1)S(1)}, bf16[256,256]{1,0:T(8,128)(2,1)S(1)}, u32[]{:S(2)}, u32[]{:S(2)}) collective-permute-start(bf16[256,256]{1,0:T(8,128)(2,1)S(1)} %bitcast.259), channel_id=1, source_target_pairs={{0,12},{2,14},{4,8},{6,10},{8,4},{10,6},{12,0},{14,2},{16,28},{18,... | collective-permute-start | bytes 393224 | tf_op jit(solution)/shard_map/ppermute | solution.py:29
  259.2 26.2 %collective-permute-start.11 = (bf16[256,256]{1,0:T(8,128)(2,1)S(1)}, bf16[256,256]{1,0:T(8,128)(2,1)S(1)}, u32[]{:S(2)}, u32[]{:S(2)}) collective-permute-start(bf16[256,256]{1,0:T(8,128)(2,1)S(1)} %bitcast.258), channel_id=1, source_target_pairs={{0,14},{2,12},{4,10},{6,8},{8,6},{10,4},{12,2},{14,0},{16,30},{18,... | collective-permute-start | bytes 393224 | tf_op jit(solution)/shard_map/ppermute | solution.py:29
  266.9 31.3 %collective-permute-start.12 = (bf16[256,256]{1,0:T(8,128)(2,1)S(1)}, bf16[256,256]{1,0:T(8,128)(2,1)S(1)}, u32[]{:S(2)}, u32[]{:S(2)}) collective-permute-start(bf16[256,256]{1,0:T(8,128)(2,1)S(1)} %bitcast.257), channel_id=1, source_target_pairs={{0,16},{2,18},{4,20},{6,22},{8,24},{10,26},{12,28},{14,30},{16,0},... | collective-permute-start | bytes 393224 | tf_op jit(solution)/shard_map/ppermute | solution.py:29
  273.0 28.1 %collective-permute-start.13 = (bf16[256,256]{1,0:T(8,128)(2,1)S(1)}, bf16[256,256]{1,0:T(8,128)(2,1)S(1)}, u32[]{:S(2)}, u32[]{:S(2)}) collective-permute-start(bf16[256,256]{1,0:T(8,128)(2,1)S(1)} %bitcast.256), channel_id=1, source_target_pairs={{0,18},{2,16},{4,22},{6,20},{8,26},{10,24},{12,30},{14,28},{16,2},... | collective-permute-start | bytes 393224 | tf_op jit(solution)/shard_map/ppermute | solution.py:29
  276.0 29.6 %collective-permute-start.14 = (bf16[256,256]{1,0:T(8,128)(2,1)S(1)}, bf16[256,256]{1,0:T(8,128)(2,1)S(1)}, u32[]{:S(2)}, u32[]{:S(2)}) collective-permute-start(bf16[256,256]{1,0:T(8,128)(2,1)S(1)} %bitcast.255), channel_id=1, source_target_pairs={{0,20},{2,22},{4,16},{6,18},{8,28},{10,30},{12,24},{14,26},{16,4},... | collective-permute-start | bytes 393224 | tf_op jit(solution)/shard_map/ppermute | solution.py:29
  280.4 30.6 %collective-permute-start.15 = (bf16[256,256]{1,0:T(8,128)(2,1)S(1)}, bf16[256,256]{1,0:T(8,128)(2,1)S(1)}, u32[]{:S(2)}, u32[]{:S(2)}) collective-permute-start(bf16[256,256]{1,0:T(8,128)(2,1)S(1)} %bitcast.254), channel_id=1, source_target_pairs={{0,22},{2,20},{4,18},{6,16},{8,30},{10,28},{12,26},{14,24},{16,6},... | collective-permute-start | bytes 393224 | tf_op jit(solution)/shard_map/ppermute | solution.py:29
  285.4 33.9 %collective-permute-start.16 = (bf16[256,256]{1,0:T(8,128)(2,1)S(1)}, bf16[256,256]{1,0:T(8,128)(2,1)S(1)}, u32[]{:S(2)}, u32[]{:S(2)}) collective-permute-start(bf16[256,256]{1,0:T(8,128)(2,1)S(1)} %bitcast.253), channel_id=1, source_target_pairs={{0,24},{2,26},{4,28},{6,30},{8,16},{10,18},{12,20},{14,22},{16,8},... | collective-permute-start | bytes 393224 | tf_op jit(solution)/shard_map/ppermute | solution.py:29
  298.3 25.2 %collective-permute-start.17 = (bf16[256,256]{1,0:T(8,128)(2,1)S(1)}, bf16[256,256]{1,0:T(8,128)(2,1)S(1)}, u32[]{:S(2)}, u32[]{:S(2)}) collective-permute-start(bf16[256,256]{1,0:T(8,128)(2,1)S(1)} %bitcast.252), channel_id=1, source_target_pairs={{0,26},{2,24},{4,30},{6,28},{8,18},{10,16},{12,22},{14,20},{16,10}... | collective-permute-start | bytes 393224 | tf_op jit(solution)/shard_map/ppermute | solution.py:29
  301.1 27.0 %collective-permute-start.18 = (bf16[256,256]{1,0:T(8,128)(2,1)S(1)}, bf16[256,256]{1,0:T(8,128)(2,1)S(1)}, u32[]{:S(2)}, u32[]{:S(2)}) collective-permute-start(bf16[256,256]{1,0:T(8,128)(2,1)S(1)} %bitcast.251), channel_id=1, source_target_pairs={{0,28},{2,30},{4,24},{6,26},{8,20},{10,22},{12,16},{14,18},{16,12}... | collective-permute-start | bytes 393224 | tf_op jit(solution)/shard_map/ppermute | solution.py:29
  305.5 27.4 %collective-permute-start.19 = (bf16[256,256]{1,0:T(8,128)(2,1)S(1)}, bf16[256,256]{1,0:T(8,128)(2,1)S(1)}, u32[]{:S(2)}, u32[]{:S(2)}) collective-permute-start(bf16[256,256]{1,0:T(8,128)(2,1)S(1)} %bitcast.250), channel_id=1, source_target_pairs={{0,30},{2,28},{4,26},{6,24},{8,22},{10,20},{12,18},{14,16},{16,14}... | collective-permute-start | bytes 393224 | tf_op jit(solution)/shard_map/ppermute | solution.py:29
  330.4 13.4 %collective-permute-start.21 = (f32[256,128]{1,0:T(8,128)S(1)}, f32[256,128]{1,0:T(8,128)S(1)}, u32[]{:S(2)}, u32[]{:S(2)}) collective-permute-start(f32[256,128]{1,0:T(8,128)S(1)} %slice_reduce_fusion), channel_id=1, source_target_pairs={{0,1},{1,0},{2,3},{3,2},{4,5},{5,4},{6,7},{7,6},{8,9},{9,8},{10,11... | collective-permute-start | bytes 393224 | tf_op jit(solution)/shard_map/ppermute | solution.py:186
  (27 other events, 109.9 us)
